TPU v7x, 32 devices: a whole 2x2x4 slice. The times are simulated.
32 devices in a mesh: strip: 8 (over z, x), chan: 4 (over y, core).
Axes of the slice: x: 2, y: 2, z: 4, core: 2. Of those that a mesh axis runs over, the one named last changes fastest.
Arguments:
- features: bfloat16 [512, 32, 128], P('chan', 'strip'), may hold values from -6 to 6
- first_filters: bfloat16 [512, 3, 3, 512], P('chan'), may hold values from -0.09375 to 0.09375
- second_filters: bfloat16 [512, 3, 3, 512], P('chan'), may hold values from -0.09375 to 0.09375
- out_grad: bfloat16 [512, 32, 128], P('chan', 'strip'), may hold values from -6 to 6
Outputs:
- output: bfloat16 [512, 32, 128], P('chan', 'strip')
- input_grad: bfloat16 [512, 32, 128], P('chan', 'strip')
- first_grad: float32 [512, 3, 3, 512], P('chan')
- second_grad: float32 [512, 3, 3, 512], P('chan')
All inputs are finite; a program needn't handle non-finite values.
Results may differ from a plain program's by a relative error of at most 0.005.
Values may be sent and summed in bfloat16 or wider, within the bound.
No kernel may reach another device: no remote copies, remote signals or barrier semaphores. Data moves between devices by JAX's collectives and lax.ppermute only.
A program may use at most 128 MiB of HBM per device.

v0:
```python
import jax
import jax.numpy as jnp
from jax import lax
from jax.sharding import PartitionSpec as P


def extended(cells, sides, width):
    for axis, dim in sides:
        count = lax.axis_size(axis)
        ends = count - 1
        head = lax.slice_in_dim(cells, 0, width, axis=dim)
        tail = lax.slice_in_dim(cells, cells.shape[dim] - width, cells.shape[dim], axis=dim)
        cells = jnp.concatenate(
            [
                lax.ppermute(tail, axis, [(i, (i + 1) % count) for i in range(ends)]),
                cells,
                lax.ppermute(head, axis, [((i + 1) % count, i) for i in range(ends)]),
            ],
            axis=dim,
        )
    return cells


def take_cols(field, shift):
    if shift == 0:
        return field
    edge = jnp.zeros(field.shape[:-1] + (1,), field.dtype)
    if shift > 0:
        return jnp.concatenate([field[..., 1:], edge], axis=-1)
    return jnp.concatenate([edge, field[..., :-1]], axis=-1)


def conv_fwd(padded, weight):
    chans, rows_pad, cols = padded.shape
    rows = rows_pad - 2
    outs = weight.shape[0]
    flat_w = weight.reshape(outs * 9, chans)
    taps = jnp.dot(
        flat_w, padded.reshape(chans, rows_pad * cols), preferred_element_type=jnp.float32
    )
    taps = taps.reshape(outs, 3, 3, rows_pad, cols)
    total = jnp.zeros((outs, rows, cols), jnp.float32)
    for kh in range(3):
        for kw in range(3):
            total = total + take_cols(taps[:, kh, kw, kh : kh + rows, :], kw - 1)
    return total


def back_stack(padded):
    outs, rows_pad, cols = padded.shape
    rows = rows_pad - 2
    pieces = []
    for kh in range(3):
        for kw in range(3):
            pieces.append(take_cols(padded[:, 2 - kh : 2 - kh + rows, :], 1 - kw))
    return jnp.stack(pieces, axis=1).reshape(outs * 9, rows * cols)


def conv_back_stacked(stacked, weight, rows, cols):
    outs = weight.shape[0]
    inner = weight.shape[3]
    flat_w = weight.reshape(outs * 9, inner)
    result = lax.dot_general(
        flat_w, stacked, (((0,), (0,)), ((), ())), preferred_element_type=jnp.float32
    )
    return result.reshape(inner, rows, cols)


def filter_grad(grad_out, padded):
    outs, rows, cols = grad_out.shape
    chans, rows_pad, _ = padded.shape
    pieces = []
    for kh in range(3):
        for kw in range(3):
            moved = take_cols(grad_out, 1 - kw)
            pieces.append(jnp.pad(moved, ((0, 0), (kh, 2 - kh), (0, 0))))
    stacked = jnp.stack(pieces, axis=1).reshape(outs * 9, rows_pad * cols)
    result = lax.dot_general(
        stacked,
        padded.reshape(chans, rows_pad * cols),
        (((1,), (1,)), ((), ())),
        preferred_element_type=jnp.float32,
    )
    return result.reshape(outs, 3, 3, chans)


def body(features, first_filters, second_filters, out_grad):
    blocks, rows, cols = features.shape
    x_pad = extended(features, (("strip", 1),), 1)
    x_all = lax.all_gather(x_pad, "chan", axis=0, tiled=True)
    pre_full = conv_fwd(x_all, first_filters)
    pre = pre_full.astype(jnp.bfloat16)
    hidden = jax.nn.silu(pre_full).astype(jnp.bfloat16)
    h_pad = extended(hidden, (("strip", 1),), 1)
    h_all = lax.all_gather(h_pad, "chan", axis=0, tiled=True)
    output = (features.astype(jnp.float32) + conv_fwd(h_all, second_filters)).astype(jnp.bfloat16)
    dy_pad = extended(out_grad, (("strip", 1),), 1)
    second_grad = filter_grad(out_grad, h_all)
    second_grad = lax.psum(second_grad, "strip")
    dy_stack = back_stack(dy_pad)
    hidden_grad = lax.psum_scatter(
        conv_back_stacked(dy_stack, second_filters, rows, cols),
        "chan",
        scatter_dimension=0,
        tiled=True,
    )
    pre_val = pre.astype(jnp.float32)
    sig = jax.nn.sigmoid(pre_val)
    pre_grad = (hidden_grad * sig * (1.0 + pre_val * (1.0 - sig))).astype(jnp.bfloat16)
    da_pad = extended(pre_grad, (("strip", 1),), 1)
    first_grad = filter_grad(pre_grad, x_all)
    da_stack = back_stack(da_pad)
    input_term = lax.psum_scatter(
        conv_back_stacked(da_stack, first_filters, rows, cols),
        "chan",
        scatter_dimension=0,
        tiled=True,
    )
    input_grad = (out_grad.astype(jnp.float32) + input_term).astype(jnp.bfloat16)
    first_grad = lax.psum(first_grad, "strip")
    return (output, input_grad, first_grad, second_grad)


def solution(mesh):
    in_specs = (
        P("chan", "strip", None),
        P("chan", None, None, None),
        P("chan", None, None, None),
        P("chan", "strip", None),
    )
    out_specs = (
        P("chan", "strip", None),
        P("chan", "strip", None),
        P("chan", None, None, None),
        P("chan", None, None, None),
    )
    return jax.shard_map(body, mesh=mesh, in_specs=in_specs, out_specs=out_specs, check_vma=False)
```

profile of v0, /device:TPU:0, one launch (start us, length us, event | category | flops | bytes accessed | tf_op | source)
XLA Modules:
  0.0 330.2 jit_solution(18411592274643033092)
XLA Ops:
  8.3 4.8 %collective-permute-start.5 = (bf16[128,1,128]{0,2,1:T(8,128)(2,1)S(1)}, bf16[128,1,128]{0,2,1:T(8,128)(2,1)S(1)}, u32[]{:S(2)}, u32[]{:S(2)}) collective-permute-start(bf16[128,1,128]{0,2,1:T(8,128)(2,1)S(1)} %get-tuple-element.34), channel_id=1, source_target_pairs={{0,4},{4,8},{8,12},{12,16},{16,20},{20,24},{24,28},{1,5},{5,9},{9,... | collective-permute-start | bytes 98312 | tf_op jit(solution)/shard_map/ppermute | solution.py:15
  16.8 5.2 %collective-permute-start = (bf16[128,1,128]{0,2,1:T(8,128)(2,1)S(1)}, bf16[128,1,128]{0,2,1:T(8,128)(2,1)S(1)}, u32[]{:S(2)}, u32[]{:S(2)}) collective-permute-start(bf16[128,1,128]{0,2,1:T(8,128)(2,1)S(1)} %get-tuple-element.28), channel_id=1, source_target_pairs={{0,4},{4,8},{8,12},{12,16},{16,20},{20,24},{24,28},{1,5},{5,9},{9,... | collective-permute-start | bytes 98312 | tf_op jit(solution)/shard_map/ppermute | solution.py:15
  22.0 2.3 copy.88
  25.3 2.7 copy.75
  28.1 2.2 reshape.51
  31.9 2.0 copy.105
  33.9 2.1 fusion.3
  37.6 8.8 %all_gather.6 = bf16[512,6,128]{0,2,1:T(8,128)(2,1)S(1)} all-gather(bf16[128,6,128]{0,2,1:T(8,128)(2,1)S(1)} %pad_maximum_fusion.1), channel_id=1, replica_groups=mesh['strip'=8,'chan'=4] {'chan'}, dimensions={0}, use_global_device_ids=true | all-gather | bytes 983040 | tf_op jit(solution)/shard_map/all_gather | solution.py:90
  46.3 3.0 convolution_bitcast_fusion.1
  49.3 5.2 %copy.76 = f32[1152,768]{1,0:T(8,128)} copy(f32[1152,768]{0,1:T(8,128)} %convolution_bitcast_fusion.1) | data formatting | bytes 7077888 | tf_op jit(solution)/shard_map/dot_general | solution.py:38
  54.5 4.8 %reshape.52 = f32[128,3,3,6,128]{4,3,2,1,0:T(8,128)} reshape(f32[1152,768]{1,0:T(8,128)} %copy.76) | data formatting | bytes 7077888 | tf_op jit(solution)/shard_map/reshape | solution.py:41
  59.4 2.3 slice_bitcast_fusion.17
  70.7 4.7 %all-reduce.49.cloned.1.call-done = f32[512,4,128]{2,1,0:T(4,128)} async-done(((f32[512,4,128]{2,1,0:T(4,128)}), f32[512,4,128]{2,1,0:T(4,128)}) %all-reduce.49.cloned.1.call-update) | async-done | bytes 1048592
  75.4 2.3 fusion.11
  79.3 4.5 %collective-permute-start.2 = (bf16[128,1,128]{2,1,0:T(2,128)(2,1)S(1)}, bf16[128,1,128]{2,1,0:T(2,128)(2,1)S(1)}, u32[]{:S(2)}, u32[]{:S(2)}) collective-permute-start(bf16[128,1,128]{2,1,0:T(2,128)(2,1)S(1)} %get-tuple-element.26), channel_id=1, source_target_pairs={{0,4},{4,8},{8,12},{12,16},{16,20},{20,24},{24,28},{1,5},{5,9},{9,... | collective-permute-start | bytes 98312 | tf_op jit(solution)/shard_map/ppermute | solution.py:15
  83.9 4.3 %collective-permute-start.7 = (bf16[128,1,128]{2,1,0:T(2,128)(2,1)S(1)}, bf16[128,1,128]{2,1,0:T(2,128)(2,1)S(1)}, u32[]{:S(2)}, u32[]{:S(2)}) collective-permute-start(bf16[128,1,128]{2,1,0:T(2,128)(2,1)S(1)} %get-tuple-element.24), channel_id=1, source_target_pairs={{0,4},{4,8},{8,12},{12,16},{16,20},{20,24},{24,28},{1,5},{5,9},{9,... | collective-permute-start | bytes 98312 | tf_op jit(solution)/shard_map/ppermute | solution.py:15
  89.8 8.7 %all_gather.7 = bf16[512,6,128]{2,0,1:T(8,128)(2,1)} all-gather(bf16[128,6,128]{2,0,1:T(8,128)(2,1)S(1)} %copy.86), channel_id=1, replica_groups=mesh['strip'=8,'chan'=4] {'chan'}, dimensions={0}, use_global_device_ids=true | all-gather | bytes 983040 | tf_op jit(solution)/shard_map/all_gather | solution.py:95
  102.8 1.8 fusion
  104.6 2.6 copy.108
  114.3 3.1 copy.109
  117.4 2.5 fusion.73
  119.9 4.0 %fusion.74 = f32[128,3,3,512]{3,0,2,1:T(8,128)} fusion(bf16[128,3,3,768]{0,3,2,1:T(8,128)(2,1)} %bitcast.64, bf16[512,768,1,1]{0,1,3,2:T(8,128)(2,1)S(1)} %bitcast.249), kind=kOutput, calls=%fused_computation.146 | convolution fusion | flops 905969664 | bytes 4915200 | tf_op jit(solution)/shard_map/dot_general | solution.py:78
  123.9 2.8 convolution_bitcast_fusion
  126.7 3.0 copy.89
  129.7 4.9 %reshape.55 = f32[128,3,3,6,128]{4,3,2,1,0:T(8,128)} reshape(f32[1152,768]{1,0:T(8,128)} %copy.89) | data formatting | bytes 7077888 | tf_op jit(solution)/shard_map/reshape | solution.py:41
  134.6 2.3 slice_bitcast_fusion.8
  137.8 2.6 fusion.23
  140.4 3.9 %all-reduce.51.cloned.1.call-done = f32[512,4,128]{2,1,0:T(4,128)} async-done(((f32[512,4,128]{2,1,0:T(4,128)}), f32[512,4,128]{2,1,0:T(4,128)}) %all-reduce.51.cloned.1.call-update) | async-done | bytes 1048592
  144.2 1.7 fusion.38
  145.9 172.9 %all-reduce.53.cloned.1.call-done = (f32[128,3,3,512]{3,0,2,1:T(8,128)}, f32[128,3,3,512]{3,0,2,1:T(8,128)}) async-done(((f32[128,3,3,512]{3,0,2,1:T(8,128)}, f32[128,3,3,512]{3,0,2,1:T(8,128)}), (f32[128,3,3,512]{3,0,2,1:T(8,128)}, f32[128,3,3,512]{3,0,2,1:T(8,128)})) %all-reduce.53.cloned.1.call-update) | async-done | bytes 4718608 | tf_op jit(solution)/shard_map/psum | solution.py:120
  318.9 3.4 %copy.185 = f32[128,3,3,512]{3,0,2,1:T(8,128)} copy(f32[128,3,3,512]{3,0,2,1:T(8,128)} %get-tuple-element.38) | data formatting | bytes 4718592
  322.3 1.4 copy.186
  (95 shorter events, 32.7 us)
Async XLA Ops:
  7.2 68.2 %all-reduce.49.cloned.1.call-start = ((), (), s32[]{:S(2)}) async-start(), calls=%async_computation | async-start | bytes 2097152
  8.3 23.2 %collective-permute-start.5 = (bf16[128,1,128]{0,2,1:T(8,128)(2,1)S(1)}, bf16[128,1,128]{0,2,1:T(8,128)(2,1)S(1)}, u32[]{:S(2)}, u32[]{:S(2)}) collective-permute-start(bf16[128,1,128]{0,2,1:T(8,128)(2,1)S(1)} %get-tuple-element.34), channel_id=1, source_target_pairs={{0,4},{4,8},{8,12},{12,16},{16,20},{20,24},{24,28},{1,5},{5,9},{9,... | collective-permute-start | bytes 98312 | tf_op jit(solution)/shard_map/ppermute | solution.py:15
  13.1 18.4 %collective-permute-start.4 = (bf16[128,1,128]{0,2,1:T(8,128)(2,1)S(1)}, bf16[128,1,128]{0,2,1:T(8,128)(2,1)S(1)}, u32[]{:S(2)}, u32[]{:S(2)}) collective-permute-start(bf16[128,1,128]{0,2,1:T(8,128)(2,1)S(1)} %get-tuple-element.35), channel_id=1, source_target_pairs={{4,0},{8,4},{12,8},{16,12},{20,16},{24,20},{28,24},{5,1},{9,5},{13... | collective-permute-start | bytes 98312 | tf_op jit(solution)/shard_map/ppermute | solution.py:17
  15.5 22.0 %collective-permute-start.1 = (bf16[128,1,128]{0,2,1:T(8,128)(2,1)S(1)}, bf16[128,1,128]{0,2,1:T(8,128)(2,1)S(1)}, u32[]{:S(2)}, u32[]{:S(2)}) collective-permute-start(bf16[128,1,128]{0,2,1:T(8,128)(2,1)S(1)} %get-tuple-element.29), channel_id=1, source_target_pairs={{4,0},{8,4},{12,8},{16,12},{20,16},{24,20},{28,24},{5,1},{9,5},{13... | collective-permute-start | bytes 98312 | tf_op jit(solution)/shard_map/ppermute | solution.py:17
  16.8 20.7 %collective-permute-start = (bf16[128,1,128]{0,2,1:T(8,128)(2,1)S(1)}, bf16[128,1,128]{0,2,1:T(8,128)(2,1)S(1)}, u32[]{:S(2)}, u32[]{:S(2)}) collective-permute-start(bf16[128,1,128]{0,2,1:T(8,128)(2,1)S(1)} %get-tuple-element.28), channel_id=1, source_target_pairs={{0,4},{4,8},{8,12},{12,16},{16,20},{20,24},{24,28},{1,5},{5,9},{9,... | collective-permute-start | bytes 98312 | tf_op jit(solution)/shard_map/ppermute | solution.py:15
  25.3 8.6 %copy-start.1 = (bf16[1152,512]{1,0:T(8,128)(2,1)}, bf16[1152,512]{1,0:T(8,128)(2,1)S(1)}, u32[]{:S(2)}) copy-start(bf16[1152,512]{1,0:T(8,128)(2,1)S(1)} %reshape.54) | copy-start | bytes 3538948
  28.0 2.2 copy-start.6
  37.4 8.9 %copy-start.2 = (bf16[1152,512]{1,0:T(8,128)(2,1)S(1)}, bf16[1152,512]{1,0:T(8,128)(2,1)}, u32[]{:S(2)}) copy-start(bf16[1152,512]{1,0:T(8,128)(2,1)} %reshape.51) | copy-start | bytes 3538948
  37.4 106.8 %all-reduce.51.cloned.1.call-start = ((), (), s32[]{:S(2)}) async-start(), calls=%async_computation.1 | async-start | bytes 2097152
  78.0 11.5 %collective-permute-start.3 = (bf16[128,1,128]{2,1,0:T(2,128)(2,1)S(1)}, bf16[128,1,128]{2,1,0:T(2,128)(2,1)S(1)}, u32[]{:S(2)}, u32[]{:S(2)}) collective-permute-start(bf16[128,1,128]{2,1,0:T(2,128)(2,1)S(1)} %get-tuple-element.27), channel_id=1, source_target_pairs={{4,0},{8,4},{12,8},{16,12},{20,16},{24,20},{28,24},{5,1},{9,5},{13... | collective-permute-start | bytes 98312 | tf_op jit(solution)/shard_map/ppermute | solution.py:17
  79.3 10.3 %collective-permute-start.2 = (bf16[128,1,128]{2,1,0:T(2,128)(2,1)S(1)}, bf16[128,1,128]{2,1,0:T(2,128)(2,1)S(1)}, u32[]{:S(2)}, u32[]{:S(2)}) collective-permute-start(bf16[128,1,128]{2,1,0:T(2,128)(2,1)S(1)} %get-tuple-element.26), channel_id=1, source_target_pairs={{0,4},{4,8},{8,12},{12,16},{16,20},{20,24},{24,28},{1,5},{5,9},{9,... | collective-permute-start | bytes 98312 | tf_op jit(solution)/shard_map/ppermute | solution.py:15
  83.9 16.0 %collective-permute-start.7 = (bf16[128,1,128]{2,1,0:T(2,128)(2,1)S(1)}, bf16[128,1,128]{2,1,0:T(2,128)(2,1)S(1)}, u32[]{:S(2)}, u32[]{:S(2)}) collective-permute-start(bf16[128,1,128]{2,1,0:T(2,128)(2,1)S(1)} %get-tuple-element.24), channel_id=1, source_target_pairs={{0,4},{4,8},{8,12},{12,16},{16,20},{20,24},{24,28},{1,5},{5,9},{9,... | collective-permute-start | bytes 98312 | tf_op jit(solution)/shard_map/ppermute | solution.py:15
  88.2 11.7 %collective-permute-start.6 = (bf16[128,1,128]{2,1,0:T(2,128)(2,1)S(1)}, bf16[128,1,128]{2,1,0:T(2,128)(2,1)S(1)}, u32[]{:S(2)}, u32[]{:S(2)}) collective-permute-start(bf16[128,1,128]{2,1,0:T(2,128)(2,1)S(1)} %get-tuple-element.25), channel_id=1, source_target_pairs={{4,0},{8,4},{12,8},{16,12},{20,16},{24,20},{28,24},{5,1},{9,5},{13... | collective-permute-start | bytes 98312 | tf_op jit(solution)/shard_map/ppermute | solution.py:17
  99.9 20.0 %copy-start = (bf16[512,6,128]{0,2,1:T(8,128)(2,1)}, bf16[512,6,128]{0,2,1:T(8,128)(2,1)S(1)}, u32[]{:S(2)}) copy-start(bf16[512,6,128]{0,2,1:T(8,128)(2,1)S(1)} %copy.87) | copy-start | bytes 2359300
  107.2 211.6 %all-reduce.53.cloned.1.call-start = ((), (), s32[]{:S(2)}) async-start(), calls=%async_computation.2 | async-start | bytes 9437184 | tf_op jit(solution)/shard_map/psum | solution.py:120
  136.9 0.9 copy-start.4
  137.3 6.9 %copy-start.5 = (bf16[128,4,128]{2,1,0:T(4,128)(2,1)S(1)}, bf16[128,4,128]{2,1,0:T(4,128)(2,1)}, u32[]{:S(2)}) copy-start(bf16[128,4,128]{2,1,0:T(4,128)(2,1)} %param.7) | copy-start | bytes 393220
  318.9 3.4 %copy-start.3 = (f32[128,3,3,512]{3,0,2,1:T(8,128)S(1)}, f32[128,3,3,512]{3,0,2,1:T(8,128)}, u32[]{:S(2)}) copy-start(f32[128,3,3,512]{3,0,2,1:T(8,128)} %get-tuple-element.39) | copy-start | bytes 7077892
Sparse Core Ops, SparseCore 0:
  37.6 37.7 all-reduce.48
  107.3 36.8 all-reduce.50
  148.5 170.3 all-reduce.52
where the time goes:
time: 331 us; the launch traced here: 330 us
  waiting for transfers between devices  182 us (55%)
  local copies, waits for them, and re-layouts  67.1 us (20%)
  starting transfers between devices  24.1 us (7%)
  blocking collectives  17.4 us (5%)
  matrix products  16.2 us (5%)
  between operations  14.8 us (4%)
  other arithmetic  8.83 us (3%)
    psum x1, waiting for transfers between devices, body(): first_grad = lax.psum(first_grad, 'strip')  173 us
    unnamed x47, local copies, waits for them, and re-layouts  25.3 us
    ppermute x4, starting transfers between devices, extended(): lax.ppermute(tail, axis, [(i, (i + 1) % count) for i in range(ends)])  18.8 us
    reshape x2, local copies, waits for them, and re-layouts, conv_fwd(): taps = taps.reshape(outs, 3, 3, rows_pad, cols)  9.68 us
    all_gather x1, blocking collectives, body(): x_all = lax.all_gather(x_pad, 'chan', axis=0, tiled=True)  8.77 us
    all_gather x1, blocking collectives, body(): h_all = lax.all_gather(h_pad, 'chan', axis=0, tiled=True)  8.68 us
    unnamed x5, waiting for transfers between devices  8.64 us
    dot_general x2, local copies, waits for them, and re-layouts, conv_fwd(): jnp.dot(flat_w, padded.reshape(chans, rows_pad * cols), preferred_element...  8.27 us
  transfers between devices with their start and end apart: 11, of which 3 were waited for; matrix products, arithmetic and copies ran while one was open for 23% of the time, Pallas kernels for 0%

commit v1 on v0

--- a/solution.py
+++ b/solution.py
@@ -117,7 +117,7 @@
         tiled=True,
     )
     input_grad = (out_grad.astype(jnp.float32) + input_term).astype(jnp.bfloat16)
-    first_grad = lax.psum(first_grad, "strip")
+    first_grad = jnp.sum(lax.all_gather(first_grad, "strip"), axis=0)
     return (output, input_grad, first_grad, second_grad)
 
 

time: 331 us -> 623 us (1.88)
  waiting for transfers between devices: 182 us -> 464 us
  other arithmetic: 8.83 us -> 20 us
    all_gather x0 -> x1, waiting for transfers between devices: none -> 346 us  [body(): first_grad = jnp.sum(lax.all_gather(first_grad, 'strip'), axis=0)]
    psum x1, waiting for transfers between devices: 173 us -> 102 us  [body(): second_grad = lax.psum(second_grad, 'strip')]
    reduce_sum x0 -> x1, other arithmetic: none -> 10.4 us  [body(): first_grad = jnp.sum(lax.all_gather(first_grad, 'strip'), axis=0)]
    unnamed x47 -> x46, local copies, waits for them, and re-layouts: 25.3 us -> 20.1 us
  transfers between devices with their start and end apart: 11 -> 12, of which waited for: 3 -> 7; matrix products, arithmetic and copies ran while one was open for 23% -> 13% of each run, Pallas kernels for 0% -> 0%
where the time goes in v1:
time: 623 us; the launch traced here: 622 us
  waiting for transfers between devices  464 us (74%)
  local copies, waits for them, and re-layouts  63.1 us (10%)
  starting transfers between devices  23.8 us (4%)
  blocking collectives  20.4 us (3%)
  other arithmetic  20 us (3%)
  matrix products  15 us (2%)
  between operations  14.8 us (2%)
    all_gather x1, waiting for transfers between devices, body(): first_grad = jnp.sum(lax.all_gather(first_grad, 'strip'), axis=0)  346 us
    psum x1, waiting for transfers between devices, body(): second_grad = lax.psum(second_grad, 'strip')  102 us
    unnamed x46, local copies, waits for them, and re-layouts  20.1 us
    ppermute x4, starting transfers between devices, extended(): lax.ppermute(tail, axis, [(i, (i + 1) % count) for i in range(ends)])  18.3 us
  transfers between devices with their start and end apart: 12, of which 7 were waited for; matrix products, arithmetic and copies ran while one was open for 13% of the time, Pallas kernels for 0%

profile of v1, /device:TPU:0, one launch (start us, length us, event | category | flops | bytes accessed | tf_op | source)
XLA Modules:
  0.0 621.7 jit_solution(15764292050677626648)
XLA Ops:
  8.3 4.8 collective-permute-start.5
  16.8 5.2 collective-permute-start
  22.0 2.3 copy.88
  25.3 2.7 copy.75
  28.1 2.2 reshape.55
  31.9 2.0 copy.105
  33.9 2.1 fusion.3
  37.5 8.8 %all_gather.9 = bf16[512,6,128]{0,2,1:T(8,128)(2,1)S(1)} all-gather(bf16[128,6,128]{0,2,1:T(8,128)(2,1)S(1)} %pad_maximum_fusion.1), channel_id=1, replica_groups=mesh['strip'=8,'chan'=4] {'chan'}, dimensions={0}, use_global_device_ids=true | all-gather | bytes 983040 | tf_op jit(solution)/shard_map/all_gather | solution.py:90
  46.3 3.0 convolution_bitcast_fusion.1
  49.2 5.2 copy.76
  54.5 4.8 reshape.56
  59.3 3.0 slice_bitcast_fusion.17
  65.0 10.3 %all-reduce.50.cloned.1.call-done = f32[512,4,128]{2,1,0:T(4,128)} async-done(((f32[512,4,128]{2,1,0:T(4,128)}), f32[512,4,128]{2,1,0:T(4,128)}) %all-reduce.50.cloned.1.call-update) | async-done | bytes 1048592
  75.3 3.0 fusion.11
  78.5 3.4 collective-permute-start.7
  83.7 4.3 collective-permute-done.6
  90.9 1.8 fusion
  92.7 2.5 copy.108
  102.5 3.1 copy.109
  105.6 2.5 fusion.73
  110.7 4.9 collective-permute-start.2
  117.8 11.7 %all_gather.10 = bf16[512,6,128]{2,0,1:T(8,128)(2,1)S(1)} all-gather(bf16[128,6,128]{2,0,1:T(8,128)(2,1)S(1)} %copy.86), channel_id=1, replica_groups=mesh['strip'=8,'chan'=4] {'chan'}, dimensions={0}, use_global_device_ids=true | all-gather | bytes 983040 | tf_op jit(solution)/shard_map/all_gather | solution.py:95
  129.7 2.5 fusion.74
  133.5 3.0 convolution_bitcast_fusion
  136.5 5.2 copy.89
  141.7 4.9 reshape.59
  146.6 2.3 slice_bitcast_fusion.8
  149.8 2.6 fusion.23
  154.1 345.6 %all-gather.3.cloned.1.call-done = f32[1024,3,3,512]{3,0,2,1:T(8,128)} async-done(((f32[128,3,3,512]{3,0,2,1:T(8,128)}), f32[1024,3,3,512]{3,0,2,1:T(8,128)}) %all-gather.3.cloned.1.call-update) | async-done | bytes 18874384 | tf_op jit(solution)/shard_map/all_gather | solution.py:120
  499.7 10.4 %reduce_sum.9 = f32[128,3,3,512]{3,0,2,1:T(8,128)} reduce(f32[8,128,3,3,512]{4,1,0,3,2:T(8,128)} %bitcast.247, f32[]{:T(128)} %constant.3.clone.1), dimensions={0}, to_apply=%region_2.3 | reduce | flops 4128768 | bytes 21233668 | tf_op jit(solution)/shard_map/reduce_sum | solution.py:120
  510.1 101.8 %all-reduce.48.cloned.1.call-done = f32[128,3,3,512]{3,0,2,1:T(8,128)} async-done(((f32[128,3,3,512]{3,0,2,1:T(8,128)}), f32[128,3,3,512]{3,0,2,1:T(8,128)}) %all-reduce.48.cloned.1.call-update) | async-done | bytes 2359312 | tf_op jit(solution)/shard_map/psum | solution.py:99
  611.9 3.3 copy.184
  (98 shorter events, 31.6 us)
Async XLA Ops:
  7.2 68.2 %all-reduce.50.cloned.1.call-start = ((), (), s32[]{:S(2)}) async-start(), calls=%async_computation.2 | async-start | bytes 2097152
  8.3 23.2 %collective-permute-start.5 = (bf16[128,1,128]{0,2,1:T(8,128)(2,1)S(1)}, bf16[128,1,128]{0,2,1:T(8,128)(2,1)S(1)}, u32[]{:S(2)}, u32[]{:S(2)}) collective-permute-start(bf16[128,1,128]{0,2,1:T(8,128)(2,1)S(1)} %get-tuple-element.32), channel_id=1, source_target_pairs={{0,4},{4,8},{8,12},{12,16},{16,20},{20,24},{24,28},{1,5},{5,9},{9,... | collective-permute-start | bytes 98312 | tf_op jit(solution)/shard_map/ppermute | solution.py:15
  13.1 18.4 %collective-permute-start.4 = (bf16[128,1,128]{0,2,1:T(8,128)(2,1)S(1)}, bf16[128,1,128]{0,2,1:T(8,128)(2,1)S(1)}, u32[]{:S(2)}, u32[]{:S(2)}) collective-permute-start(bf16[128,1,128]{0,2,1:T(8,128)(2,1)S(1)} %get-tuple-element.33), channel_id=1, source_target_pairs={{4,0},{8,4},{12,8},{16,12},{20,16},{24,20},{28,24},{5,1},{9,5},{13... | collective-permute-start | bytes 98312 | tf_op jit(solution)/shard_map/ppermute | solution.py:17
  15.5 22.0 %collective-permute-start.1 = (bf16[128,1,128]{0,2,1:T(8,128)(2,1)S(1)}, bf16[128,1,128]{0,2,1:T(8,128)(2,1)S(1)}, u32[]{:S(2)}, u32[]{:S(2)}) collective-permute-start(bf16[128,1,128]{0,2,1:T(8,128)(2,1)S(1)} %get-tuple-element.27), channel_id=1, source_target_pairs={{4,0},{8,4},{12,8},{16,12},{20,16},{24,20},{28,24},{5,1},{9,5},{13... | collective-permute-start | bytes 98312 | tf_op jit(solution)/shard_map/ppermute | solution.py:17
  16.8 20.7 %collective-permute-start = (bf16[128,1,128]{0,2,1:T(8,128)(2,1)S(1)}, bf16[128,1,128]{0,2,1:T(8,128)(2,1)S(1)}, u32[]{:S(2)}, u32[]{:S(2)}) collective-permute-start(bf16[128,1,128]{0,2,1:T(8,128)(2,1)S(1)} %get-tuple-element.26), channel_id=1, source_target_pairs={{0,4},{4,8},{8,12},{12,16},{16,20},{20,24},{24,28},{1,5},{5,9},{9,... | collective-permute-start | bytes 98312 | tf_op jit(solution)/shard_map/ppermute | solution.py:15
  25.3 8.6 %copy-start = (bf16[1152,512]{1,0:T(8,128)(2,1)}, bf16[1152,512]{1,0:T(8,128)(2,1)S(1)}, u32[]{:S(2)}) copy-start(bf16[1152,512]{1,0:T(8,128)(2,1)S(1)} %reshape.58) | copy-start | bytes 3538948
  28.0 2.2 copy-start.6
  37.3 8.9 %copy-start.2 = (bf16[1152,512]{1,0:T(8,128)(2,1)S(1)}, bf16[1152,512]{1,0:T(8,128)(2,1)}, u32[]{:S(2)}) copy-start(bf16[1152,512]{1,0:T(8,128)(2,1)} %reshape.55) | copy-start | bytes 3538948
  37.4 115.0 %all-reduce.52.cloned.1.call-start = ((), (), s32[]{:S(2)}) async-start(), calls=%async_computation.3 | async-start | bytes 2097152
  78.5 5.3 collective-permute-start.7
  81.9 6.2 collective-permute-start.6
  95.3 404.4 %all-gather.3.cloned.1.call-start = ((), (), s32[]{:S(2)}) async-start(), calls=%async_computation.1 | async-start | bytes 21233664 | tf_op jit(solution)/shard_map/all_gather | solution.py:120
  108.2 1.0 copy-start.3
  108.2 503.7 %all-reduce.48.cloned.1.call-start = ((), (), s32[]{:S(2)}) async-start(), calls=%async_computation | async-start | bytes 4718592 | tf_op jit(solution)/shard_map/psum | solution.py:99
  109.4 6.5 %collective-permute-start.3 = (bf16[128,1,128]{2,1,0:T(2,128)(2,1)S(1)}, bf16[128,1,128]{2,1,0:T(2,128)(2,1)S(1)}, u32[]{:S(2)}, u32[]{:S(2)}) collective-permute-start(bf16[128,1,128]{2,1,0:T(2,128)(2,1)S(1)} %get-tuple-element.25), channel_id=1, source_target_pairs={{4,0},{8,4},{12,8},{16,12},{20,16},{24,20},{28,24},{5,1},{9,5},{13... | collective-permute-start | bytes 98312 | tf_op jit(solution)/shard_map/ppermute | solution.py:17
  110.7 6.8 %collective-permute-start.2 = (bf16[128,1,128]{2,1,0:T(2,128)(2,1)S(1)}, bf16[128,1,128]{2,1,0:T(2,128)(2,1)S(1)}, u32[]{:S(2)}, u32[]{:S(2)}) collective-permute-start(bf16[128,1,128]{2,1,0:T(2,128)(2,1)S(1)} %get-tuple-element.24), channel_id=1, source_target_pairs={{0,4},{4,8},{8,12},{12,16},{16,20},{20,24},{24,28},{1,5},{5,9},{9,... | collective-permute-start | bytes 98312 | tf_op jit(solution)/shard_map/ppermute | solution.py:15
  132.2 1.3 copy-start.1
  148.9 0.9 copy-start.4
  149.3 3.1 copy-start.5
Sparse Core Ops, SparseCore 0:
  37.5 37.7 all-reduce.49
  95.4 38.7 all-reduce.51
  136.3 363.3 all-gather.2
  503.1 108.6 all-reduce.47
